TPU v7x, 256 devices: a whole 4x4x8 slice. The times are simulated.
256 devices in a mesh: dp: 16 (over z_lo, x), tensor: 16 (over z_hi, y, core).
Axes of the slice: x: 4, y: 4, z: 8 (z_hi: 2, z_lo: 4; z = z_hi * 4 + z_lo), core: 2. Of those that a mesh axis runs over, the one named last changes fastest.
Arguments:
- cotangent: bfloat16 [8192, 4096], P(('dp', 'tensor')), may hold values from -6 to 6
- gate: bfloat16 [8192, 14336], P('dp', 'tensor'), may hold values from -8 to 8
- up: bfloat16 [8192, 14336], P('dp', 'tensor'), may hold values from -6 to 6
- w_down: bfloat16 [4, 14336, 4096], P(None, 'tensor', 'dp'), may hold values from -0.03125 to 0.03125
- language: int32 [16], replicated, may hold values from 0 to 3
Outputs:
- d_gate: bfloat16 [8192, 14336], P('dp', 'tensor')
- d_up: bfloat16 [8192, 14336], P('dp', 'tensor')
- d_weight: float32 [4, 14336, 4096], P(None, 'tensor', 'dp')
All inputs are finite; a program needn't handle non-finite values.
Results may differ from a plain program's by a relative error of at most 0.0029.
Values may be sent and summed in bfloat16 or wider, within the bound.
No kernel may reach another device: no remote copies, remote signals or barrier semaphores. Data moves between devices by JAX's collectives and lax.ppermute only.
A program may use at most 128 MiB of HBM per device.

v0:
```python
import jax
import jax.numpy as jnp
from jax import lax
from jax.sharding import PartitionSpec as P


def shards(cotangent, gate, up, w_down, language):
    groups = lax.axis_size("dp")
    variants = w_down.shape[0]
    ff_dev = w_down.shape[1]
    feat_dev = w_down.shape[2]
    out_rows = lax.all_gather(cotangent, "tensor", axis=0, tiled=True)
    gate_f = gate.astype(jnp.float32)
    up_f = up.astype(jnp.float32)
    sig = jax.nn.sigmoid(gate_f)
    act = gate_f * sig
    hidden = (act * up_f).astype(jnp.bfloat16)
    slabs = jnp.take(w_down, language, axis=0)
    received = lax.all_to_all(slabs, "dp", split_axis=0, concat_axis=2, tiled=True)
    weights = received[0]
    d_hidden = lax.dot_general(
        out_rows, weights, (((1,), (1,)), ((), ())), preferred_element_type=jnp.float32
    )
    d_up = (d_hidden * act).astype(jnp.bfloat16)
    d_gate = (d_hidden * up_f * sig * (1.0 + gate_f * (1.0 - sig))).astype(jnp.bfloat16)
    selector = (language[None, :] == jnp.arange(variants, dtype=jnp.int32)[:, None]).astype(
        jnp.float32
    )
    partial_term = lax.dot_general(
        hidden, out_rows, (((0,), (0,)), ((), ())), preferred_element_type=jnp.float32
    )
    pieces = lax.all_to_all(
        partial_term.reshape(ff_dev, groups, feat_dev),
        "dp",
        split_axis=1,
        concat_axis=1,
        tiled=True,
    )
    d_weight = jnp.einsum("lg,fgd->lfd", selector, pieces, precision=lax.Precision.HIGHEST)
    return (d_gate, d_up, d_weight)


def solution(mesh):
    return jax.shard_map(
        shards,
        mesh=mesh,
        in_specs=(
            P(("dp", "tensor"), None),
            P("dp", "tensor"),
            P("dp", "tensor"),
            P(None, "tensor", "dp"),
            P(),
        ),
        out_specs=(P("dp", "tensor"), P("dp", "tensor"), P(None, "tensor", "dp")),
        check_vma=False,
    )
```

profile of v0, /device:TPU:64, one launch (start us, length us, event | category | flops | bytes accessed | tf_op | source)
XLA Modules:
  0.0 566.6 jit_solution(13106661074899269644)
XLA Ops:
  7.2 0.0 copy-start
  7.2 0.8 compare_and_fusion
  8.0 0.7 compare_select_fusion
  8.6 0.0 copy-done
  8.7 4.0 gather_fusion
  12.7 6.9 %broadcast_select_fusion = bf16[16,896,256]{2,1,0:T(8,128)(2,1)} fusion(bf16[16,896,256]{2,1,0:T(8,128)(2,1)} %gather_fusion, pred[16]{0:T(512)(128)(4,1)S(1)} %compare_and_fusion), kind=kLoop, calls=%fused_computation.4 | loop fusion | flops 3670016 | bytes 14680080 | tf_op jit(solution)/shard_map/jit(_take)/select_n | solution.py:18
  19.6 0.0 copy-start.2
  19.6 0.0 copy-start.3
  19.6 8.2 %all-to-all-start = ((bf16[16,896,256]{2,1,0:T(8,128)(2,1)}), bf16[16,896,256]{2,1,0:T(8,128)(2,1)}, u32[]{:S(2)}, u32[]{:S(2)}) async-start(bf16[16,896,256]{2,1,0:T(8,128)(2,1)} %broadcast_select_fusion), calls=%async_computation | async-start | bytes 14680064 | tf_op jit(solution)/shard_map/all_to_all | solution.py:19
  27.7 0.0 all-gather.2.cloned.1.call-start
  27.8 0.7 all-gather.2.cloned.1.call-update
  28.5 0.0 copy-done.2
  28.5 0.5 copy.26
  29.0 0.0 copy-done.3
  29.0 0.5 copy.25
  29.6 121.4 %all-gather.2.cloned.1.call-done = bf16[512,4096]{1,0:T(8,128)(2,1)} async-done(((bf16[32,4096]{1,0:T(8,128)(2,1)}), bf16[512,4096]{1,0:T(8,128)(2,1)}) %all-gather.2.cloned.1.call-update) | async-done | bytes 4194320 | tf_op jit(solution)/shard_map/all_gather | solution.py:12
  150.9 9.5 %fusion.11 = f32[896,4096]{1,0:T(8,128)} fusion(bf16[512,4096]{1,0:T(8,128)(2,1)} %all-gather.2.cloned.1.call-done, bf16[512,896]{0,1:T(8,128)(2,1)S(1)} %copy.25, bf16[512,896]{0,1:T(8,128)(2,1)S(1)} %copy.26), kind=kOutput, calls=%fused_computation.20 | convolution fusion | flops 3761766400 | bytes 20709376 | tf_op jit(solution)/shard_map/dot_general | solution.py:29
  160.4 12.0 %copy.36 = f32[112,16,8,256]{3,2,0,1:T(8,128)} copy(f32[112,16,8,256]{3,2,1,0:T(8,128)} %bitcast.20) | data formatting | bytes 29360128 | tf_op jit(solution)/shard_map/reshape | solution.py:33
  172.4 44.2 %all-to-all-done = bf16[16,896,256]{2,1,0:T(8,128)(2,1)} async-done(((bf16[16,896,256]{2,1,0:T(8,128)(2,1)}), bf16[16,896,256]{2,1,0:T(8,128)(2,1)}, u32[]{:S(2)}, u32[]{:S(2)}) %all-to-all-start) | async-done | bytes 7340064 | tf_op jit(solution)/shard_map/all_to_all | solution.py:19
  216.6 5.2 all-to-all-start.1
  221.7 11.1 %copy.24 = bf16[1,896,16,256]{1,3,2,0:T(8,128)(2,1)} copy(bf16[1,896,16,256]{3,1,2,0:T(8,128)(2,1)} %bitcast.1) | data formatting | bytes 14680064 | tf_op jit(solution)/shard_map/all_to_all | solution.py:19
  232.9 9.8 %fusion.10 = (bf16[512,896]{0,1:T(8,128)(2,1)}, bf16[512,896]{0,1:T(8,128)(2,1)S(1)}) fusion(bf16[512,896]{0,1:T(8,128)(2,1)S(1)} %copy.26, bf16[512,896]{0,1:T(8,128)(2,1)S(1)} %copy.25, bf16[896,4096]{0,1:T(8,128)(2,1)} %bitcast.21, bf16[512,4096]{1,0:T(8,128)(2,1)} %all-gather.2.cloned.1.call-done), kind=kOutput, calls=%fused_computation.19 | convolution fusion | flops 3764977664 | bytes 15204352 | tf_op jit(solution)/shard_map/dot_general | solution.py:21
  242.7 0.0 copy-start.4
  242.7 2.2 copy.30
  244.9 1.3 copy.29
  246.2 292.8 %all-to-all-done.1 = f32[896,16,256]{2,0,1:T(8,128)} async-done(((f32[896,16,256]{2,0,1:T(8,128)}), f32[896,16,256]{2,0,1:T(8,128)}, u32[]{:S(2)}, u32[]{:S(2)}) %all-to-all-start.1) | async-done | bytes 14680096 | tf_op jit(solution)/shard_map/all_to_all | solution.py:32
  539.0 0.0 copy-done.4
  539.0 0.0 copy-start.1
  539.0 18.3 %fusion = f32[4,896,256]{2,0,1:T(4,128)S(1)} fusion(f32[896,16,256]{2,0,1:T(8,128)} %all-to-all-done.1, s32[16]{0:T(128)S(1)} %copy-done.4), kind=kOutput, calls=%fused_computation.2 | convolution fusion | flops 176160832 | bytes 18350144 | tf_op jit(solution)/shard_map/lg,fgd->lfd/dot_general | solution.py:39
  557.3 2.5 copy.31
  559.8 0.0 copy-done.1
  (1 shorter events, 0.0 us)
Async XLA Ops:
  7.2 1.5 copy-start
  19.6 8.9 %copy-start.2 = (bf16[512,896]{1,0:T(8,128)(2,1)S(1)}, bf16[512,896]{1,0:T(8,128)(2,1)}, u32[]{:S(2)}) copy-start(bf16[512,896]{1,0:T(8,128)(2,1)} %param.6) | copy-start | bytes 2752516
  19.6 9.4 %copy-start.3 = (bf16[512,896]{1,0:T(8,128)(2,1)S(1)}, bf16[512,896]{1,0:T(8,128)(2,1)}, u32[]{:S(2)}) copy-start(bf16[512,896]{1,0:T(8,128)(2,1)} %param.7) | copy-start | bytes 2752516
  19.6 197.0 %all-to-all-start = ((bf16[16,896,256]{2,1,0:T(8,128)(2,1)}), bf16[16,896,256]{2,1,0:T(8,128)(2,1)}, u32[]{:S(2)}, u32[]{:S(2)}) async-start(bf16[16,896,256]{2,1,0:T(8,128)(2,1)} %broadcast_select_fusion), calls=%async_computation | async-start | bytes 14680064 | tf_op jit(solution)/shard_map/all_to_all | solution.py:19
  27.7 123.2 %all-gather.2.cloned.1.call-start = ((), (), s32[]{:S(2)}) async-start(), calls=%async_computation.2 | async-start | bytes 4456448 | tf_op jit(solution)/shard_map/all_gather | solution.py:12
  216.6 322.4 %all-to-all-start.1 = ((f32[896,16,256]{2,0,1:T(8,128)}), f32[896,16,256]{2,0,1:T(8,128)}, u32[]{:S(2)}, u32[]{:S(2)}) async-start(f32[896,16,256]{2,0,1:T(8,128)} %bitcast.19), calls=%async_computation.1 | async-start | bytes 29360128 | tf_op jit(solution)/shard_map/all_to_all | solution.py:32
  242.7 296.3 %copy-start.4 = (s32[16]{0:T(128)S(1)}, s32[16]{0:T(128)}, u32[]{:S(2)}) copy-start(s32[16]{0:T(128)} %param.9) | copy-start | bytes 196
  539.0 20.8 %copy-start.1 = (bf16[4,896,256]{2,1,0:T(8,128)(2,1)S(1)}, bf16[4,896,256]{2,1,0:T(8,128)(2,1)}, u32[]{:S(2)}) copy-start(bf16[4,896,256]{2,1,0:T(8,128)(2,1)} %param.8) | copy-start | bytes 5505028
Sparse Core Ops, SparseCore 0:
  31.3 119.5 all-gather.1
where the time goes:
time: 567 us
  waiting for transfers between devices  459 us (81%)
  matrix products  37.6 us (7%)
  local copies, waits for them, and re-layouts  34.2 us (6%)
  between operations  14.1 us (2%)
  starting transfers between devices  13.4 us (2%)
  other arithmetic  8.33 us (1%)
    all_to_all x1, waiting for transfers between devices, shards(): lax.all_to_all(partial_term.reshape(ff_dev, groups, feat_dev), 'dp', spli...  293 us
    all_gather x1, waiting for transfers between devices, shards(): out_rows = lax.all_gather(cotangent, 'tensor', axis=0, tiled=True)  121 us
    all_to_all x1, waiting for transfers between devices, shards(): lax.all_to_all(slabs, 'dp', split_axis=0, concat_axis=2, tiled=True)  44.2 us
    dot_general x1, matrix products, shards(): jnp.einsum('lg,fgd->lfd', selector, pieces, precision=lax.Precision.HIGHEST)  18.3 us
    reshape x1, local copies, waits for them, and re-layouts, shards(): partial_term.reshape(ff_dev, groups, feat_dev)  12 us
  transfers between devices with their start and end apart: 3, of which 3 were waited for; matrix products, arithmetic and copies ran while one was open for 8% of the time, Pallas kernels for 0%

commit v1 on v0

--- a/solution.py
+++ b/solution.py
@@ -2,6 +2,11 @@
 import jax.numpy as jnp
 from jax import lax
 from jax.sharding import PartitionSpec as P
+
+
+def gather_over(x, name, dim):
+    sent = jnp.stack([x] * lax.axis_size(name))
+    return jnp.concatenate(lax.all_to_all(sent, name, 0, 0), axis=dim)
 
 
 def shards(cotangent, gate, up, w_down, language):
@@ -9,7 +14,7 @@
     variants = w_down.shape[0]
     ff_dev = w_down.shape[1]
     feat_dev = w_down.shape[2]
-    out_rows = lax.all_gather(cotangent, "tensor", axis=0, tiled=True)
+    out_rows = gather_over(cotangent, "tensor", 0)
     gate_f = gate.astype(jnp.float32)
     up_f = up.astype(jnp.float32)
     sig = jax.nn.sigmoid(gate_f)

time: 567 us -> 631 us (1.11); the launches traced: 567 us -> 623 us
  waiting for transfers between devices: 459 us -> 524 us
  between operations: 14.1 us -> 0.72 us
  starting transfers between devices: 13.4 us -> 21.4 us
    all_gather x1 -> x0, waiting for transfers between devices: 121 us -> none  [shards(): out_rows = lax.all_gather(cotangent, 'tensor', axis=0, tiled=True)]
    all_to_all x1, waiting for transfers between devices: 44.2 us -> 143 us  [shards(): lax.all_to_all(slabs, 'dp', split_axis=0, concat_axis=2, tiled=True)]
    all_to_all x0 -> x1, waiting for transfers between devices: none -> 88.4 us  [gather_over(): return jnp.concatenate(lax.all_to_all(sent, name, 0, 0), axis=dim)]
    reshape x1 -> x0, local copies, waits for them, and re-layouts: 12 us -> none  [shards(): partial_term.reshape(ff_dev, groups, feat_dev)]
    all_to_all x0 -> x1, starting transfers between devices: none -> 9.58 us  [gather_over(): return jnp.concatenate(lax.all_to_all(sent, name, 0, 0), axis=dim)]
    dot_general x0 -> x1, local copies, waits for them, and re-layouts: none -> 6.62 us  [shards(): lax.dot_general(hidden, out_rows, (((0,), (0,)), ((), ())), preferred_ele...]
where the time goes in v1:
time: 631 us; the launch traced here: 623 us
  waiting for transfers between devices  524 us (83%)
  matrix products  37.6 us (6%)
  local copies, waits for them, and re-layouts  32.3 us (5%)
  starting transfers between devices  21.4 us (3%)
  other arithmetic  6.79 us (1%)
    all_to_all x1, waiting for transfers between devices, shards(): lax.all_to_all(partial_term.reshape(ff_dev, groups, feat_dev), 'dp', spli...  293 us
    all_to_all x1, waiting for transfers between devices, shards(): lax.all_to_all(slabs, 'dp', split_axis=0, concat_axis=2, tiled=True)  143 us
    all_to_all x1, waiting for transfers between devices, gather_over(): return jnp.concatenate(lax.all_to_all(sent, name, 0, 0), axis=dim)  88.4 us
    dot_general x1, matrix products, shards(): jnp.einsum('lg,fgd->lfd', selector, pieces, precision=lax.Precision.HIGHEST)  18.3 us
  transfers between devices with their start and end apart: 3, of which 3 were waited for; matrix products, arithmetic and copies ran while one was open for 8% of the time, Pallas kernels for 0%

profile of v1, /device:TPU:64, one launch (start us, length us, event | category | flops | bytes accessed | tf_op | source)
XLA Modules:
  0.0 623.3 jit_solution(1740007196001290812)
XLA Ops:
  0.6 0.0 copy-start
  0.6 3.5 stack.2
  4.2 0.0 copy-start.4
  4.2 9.6 %all-to-all-start.1 = ((bf16[16,32,4096]{2,1,0:T(8,128)(2,1)}), bf16[16,32,4096]{2,1,0:T(8,128)(2,1)}, u32[]{:S(2)}, u32[]{:S(2)}) async-start(bf16[16,32,4096]{2,1,0:T(8,128)(2,1)} %stack.2), calls=%async_computation.1 | async-start | bytes 8388608 | tf_op jit(solution)/shard_map/all_to_all | solution.py:9
  13.8 0.0 copy-done.4
  13.8 0.0 copy-done
  13.8 3.9 gather_fusion
  17.8 6.8 %broadcast_select_fusion = bf16[16,896,256]{2,1,0:T(8,128)(2,1)} fusion(bf16[16,896,256]{2,1,0:T(8,128)(2,1)} %gather_fusion, pred[16]{0:T(512)(128)(4,1)S(1)} %compare_and_fusion), kind=kLoop, calls=%fused_computation.3 | loop fusion | flops 3670016 | bytes 14680080 | tf_op jit(solution)/shard_map/jit(_take)/select_n | solution.py:23
  24.5 0.0 copy-start.2
  24.5 0.0 copy-start.3
  24.6 88.4 %all-to-all-done.1 = bf16[16,32,4096]{2,1,0:T(8,128)(2,1)} async-done(((bf16[16,32,4096]{2,1,0:T(8,128)(2,1)}), bf16[16,32,4096]{2,1,0:T(8,128)(2,1)}, u32[]{:S(2)}, u32[]{:S(2)}) %all-to-all-start.1) | async-done | bytes 4194336 | tf_op jit(solution)/shard_map/all_to_all | solution.py:9
  113.0 6.7 %all-to-all-start = ((bf16[16,896,256]{2,1,0:T(8,128)(2,1)}), bf16[16,896,256]{2,1,0:T(8,128)(2,1)}, u32[]{:S(2)}, u32[]{:S(2)}) async-start(bf16[16,896,256]{2,1,0:T(8,128)(2,1)} %broadcast_select_fusion), calls=%async_computation | async-start | bytes 14680064 | tf_op jit(solution)/shard_map/all_to_all | solution.py:24
  119.6 0.0 copy-done.2
  119.6 0.5 copy.28
  120.2 0.0 copy-done.3
  120.2 0.5 copy.27
  120.7 6.6 %copy.29 = bf16[4096,512]{1,0:T(8,128)(2,1)} copy(bf16[4096,512]{0,1:T(8,128)(2,1)} %bitcast.7) | data formatting | bytes 8388608 | tf_op jit(solution)/shard_map/dot_general | solution.py:34
  127.3 9.5 %fusion.12 = f32[896,16,256]{2,0,1:T(8,128)} fusion(bf16[16,256,512]{2,1,0:T(8,128)(2,1)} %bitcast.23, bf16[512,896]{0,1:T(8,128)(2,1)S(1)} %copy.27, bf16[512,896]{0,1:T(8,128)(2,1)S(1)} %copy.28), kind=kOutput, calls=%fused_computation.20 | convolution fusion | flops 3761766400 | bytes 20709376 | tf_op jit(solution)/shard_map/dot_general | solution.py:34
  136.8 143.3 %all-to-all-done = bf16[16,896,256]{2,1,0:T(8,128)(2,1)} async-done(((bf16[16,896,256]{2,1,0:T(8,128)(2,1)}), bf16[16,896,256]{2,1,0:T(8,128)(2,1)}, u32[]{:S(2)}, u32[]{:S(2)}) %all-to-all-start) | async-done | bytes 7340064 | tf_op jit(solution)/shard_map/all_to_all | solution.py:24
  280.1 5.2 all-to-all-start.2
  285.3 11.2 %copy.26 = bf16[1,896,16,256]{1,3,2,0:T(8,128)(2,1)} copy(bf16[1,896,16,256]{3,1,2,0:T(8,128)(2,1)} %bitcast.1) | data formatting | bytes 14680064 | tf_op jit(solution)/shard_map/all_to_all | solution.py:24
  296.4 9.8 %fusion.10 = (bf16[512,896]{0,1:T(8,128)(2,1)}, bf16[512,896]{0,1:T(8,128)(2,1)S(1)}) fusion(bf16[512,896]{0,1:T(8,128)(2,1)S(1)} %copy.28, bf16[512,896]{0,1:T(8,128)(2,1)S(1)} %copy.27, bf16[896,4096]{0,1:T(8,128)(2,1)} %bitcast.22, bf16[512,4096]{1,0:T(8,128)(2,1)} %bitcast.3), kind=kOutput, calls=%fused_computation.18 | convolution fusion | flops 3764977664 | bytes 15204352 | tf_op jit(solution)/shard_map/dot_general | solution.py:26
  306.3 2.2 copy.32
  308.5 1.3 copy.31
  309.7 292.8 %all-to-all-done.2 = f32[896,16,256]{2,0,1:T(8,128)} async-done(((f32[896,16,256]{2,0,1:T(8,128)}), f32[896,16,256]{2,0,1:T(8,128)}, u32[]{:S(2)}, u32[]{:S(2)}) %all-to-all-start.2) | async-done | bytes 14680096 | tf_op jit(solution)/shard_map/all_to_all | solution.py:37
  602.5 0.0 copy-start.1
  602.5 18.3 %fusion = f32[4,896,256]{2,0,1:T(4,128)S(1)} fusion(f32[896,16,256]{2,0,1:T(8,128)} %all-to-all-done.2, s32[16]{0:T(128)S(1)} %copy-done.4), kind=kOutput, calls=%fused_computation.1 | convolution fusion | flops 176160832 | bytes 18350144 | tf_op jit(solution)/shard_map/lg,fgd->lfd/dot_general | solution.py:44
  620.8 2.5 copy.33
  623.3 0.0 copy-done.1
  (3 shorter events, 0.0 us)
Async XLA Ops:
  0.6 13.2 %copy-start = (bf16[4,896,256]{2,1,0:T(8,128)(2,1)S(1)}, bf16[4,896,256]{2,1,0:T(8,128)(2,1)}, u32[]{:S(2)}) copy-start(bf16[4,896,256]{2,1,0:T(8,128)(2,1)} %param.8) | copy-start | bytes 5505028
  4.2 9.6 %copy-start.4 = (s32[16]{0:T(128)S(1)}, s32[16]{0:T(128)}, u32[]{:S(2)}) copy-start(s32[16]{0:T(128)} %param.9) | copy-start | bytes 196
  4.2 108.8 %all-to-all-start.1 = ((bf16[16,32,4096]{2,1,0:T(8,128)(2,1)}), bf16[16,32,4096]{2,1,0:T(8,128)(2,1)}, u32[]{:S(2)}, u32[]{:S(2)}) async-start(bf16[16,32,4096]{2,1,0:T(8,128)(2,1)} %stack.2), calls=%async_computation.1 | async-start | bytes 8388608 | tf_op jit(solution)/shard_map/all_to_all | solution.py:9
  24.5 95.1 %copy-start.2 = (bf16[512,896]{1,0:T(8,128)(2,1)S(1)}, bf16[512,896]{1,0:T(8,128)(2,1)}, u32[]{:S(2)}) copy-start(bf16[512,896]{1,0:T(8,128)(2,1)} %param.6) | copy-start | bytes 2752516
  24.5 95.6 %copy-start.3 = (bf16[512,896]{1,0:T(8,128)(2,1)S(1)}, bf16[512,896]{1,0:T(8,128)(2,1)}, u32[]{:S(2)}) copy-start(bf16[512,896]{1,0:T(8,128)(2,1)} %param.7) | copy-start | bytes 2752516
  113.0 167.2 %all-to-all-start = ((bf16[16,896,256]{2,1,0:T(8,128)(2,1)}), bf16[16,896,256]{2,1,0:T(8,128)(2,1)}, u32[]{:S(2)}, u32[]{:S(2)}) async-start(bf16[16,896,256]{2,1,0:T(8,128)(2,1)} %broadcast_select_fusion), calls=%async_computation | async-start | bytes 14680064 | tf_op jit(solution)/shard_map/all_to_all | solution.py:24
  280.1 322.4 %all-to-all-start.2 = ((f32[896,16,256]{2,0,1:T(8,128)}), f32[896,16,256]{2,0,1:T(8,128)}, u32[]{:S(2)}, u32[]{:S(2)}) async-start(f32[896,16,256]{2,0,1:T(8,128)} %fusion.12), calls=%async_computation.2 | async-start | bytes 29360128 | tf_op jit(solution)/shard_map/all_to_all | solution.py:37
  602.5 20.8 %copy-start.1 = (bf16[4,896,256]{2,1,0:T(8,128)(2,1)S(1)}, bf16[4,896,256]{2,1,0:T(8,128)(2,1)}, u32[]{:S(2)}) copy-start(bf16[4,896,256]{2,1,0:T(8,128)(2,1)} %param.8) | copy-start | bytes 5505028
